TPU v7x, 32 devices: a whole 2x2x4 slice. The times are simulated.
32 devices in a mesh: groups: 2 (over x), state: 16 (over z, y, core).
Axes of the slice: x: 2, y: 2, z: 4, core: 2. Of those that a mesh axis runs over, the one named last changes fastest.
Arguments:
- forward_probs: float32 [256, 8, 8192], P('groups', None, 'state'), parts along dimension 0, may hold values from 0.1 to 10
- token_ids: int32 [256, 8], P('groups'), parts along dimension 0, may hold values from 0 to 16383
- transition: bfloat16 [8192, 8192], P('state'), may hold values from 0.1 to 10
- emission: bfloat16 [8192, 16384], P('state'), may hold values from 0.05 to 20
Outputs:
- backward_probs: float32 [256, 8, 8192], P('groups', None, 'state'), parts along dimension 0
- trans_counts: float32 [16384, 8192], P(('groups', 'state')), parts along dimension 0
There are 2 independent parts, one for each index of `groups`. A program takes and returns all parts, laid end to end along the dimension named above; an argument that names none is the same for every part. Nothing has to cross between parts.
All inputs are finite; a program needn't handle non-finite values.
Results may differ from a plain program's by a relative error of at most 0.00031.
Values may be sent and summed in bfloat16 or wider, within the bound.
No kernel may reach another device: no remote copies, remote signals or barrier semaphores. Data moves between devices by JAX's collectives and lax.ppermute only.
A program may use at most 192 MiB of HBM per device.

v0:
```python
import jax
import jax.numpy as jnp
from jax import lax
from jax.sharding import PartitionSpec as P


def on_device(forward_probs, token_ids, transition, emission):
    state_rows = transition.shape[0]
    states = transition.shape[1]
    seq_count = token_ids.shape[0]
    step_count = token_ids.shape[1]
    emitted = jnp.take(emission, token_ids.reshape(-1), axis=1).astype(jnp.float32)
    emitted = emitted.reshape(state_rows, seq_count, step_count)
    backward = jnp.ones((seq_count, state_rows), jnp.float32)
    weighted = (emitted[:, :, step_count - 1].T * backward).astype(jnp.bfloat16)
    backs = [backward]
    stored = []
    scales = []
    for t in range(step_count - 2, -1, -1):
        whole = lax.all_gather(weighted, "state", axis=1, tiled=True)
        scale_sum = lax.psum(jnp.sum(weighted.astype(jnp.float32), axis=1), "state")
        product = lax.dot_general(
            whole, transition, (((1,), (1,)), ((), ())), preferred_element_type=jnp.float32
        )
        backward = product / scale_sum[:, None]
        stored.append(whole)
        scales.append(scale_sum)
        backs.append(backward)
        if t > 0:
            weighted = (emitted[:, :, t].T * backward).astype(jnp.bfloat16)
    backs = backs[::-1]
    stored = stored[::-1]
    scales = scales[::-1]
    backward_probs = jnp.stack(backs, axis=1)
    partial_norms = jnp.sum(
        forward_probs[:, : step_count - 1, :] * backward_probs[:, : step_count - 1, :], axis=2
    )
    norm_sums = lax.psum(partial_norms, "state")
    shares = []
    for t in range(step_count - 1):
        shares.append(
            (forward_probs[:, t, :] / (scales[t] * norm_sums[:, t])[:, None]).astype(jnp.bfloat16)
        )
    share_mat = jnp.concatenate(shares, axis=0)
    vector_mat = jnp.concatenate(stored, axis=0)
    moments = lax.dot_general(
        share_mat, vector_mat, (((0,), (0,)), ((), ())), preferred_element_type=jnp.float32
    )
    factor = float(states) * float(states) / float(seq_count * (step_count - 1))
    trans_counts = transition.astype(jnp.float32) * moments * factor
    return (backward_probs, trans_counts)


def solution(mesh):
    placed = (P("groups", None, "state"), P("groups", None), P("state", None), P("state", None))
    return jax.shard_map(
        on_device,
        mesh=mesh,
        in_specs=placed,
        out_specs=(P("groups", None, "state"), P(("groups", "state"), None)),
        check_vma=False,
    )
```

profile of v0, /device:TPU:0, one launch (start us, length us, event | category | flops | bytes accessed | tf_op | source)
XLA Modules:
  0.0 467.3 jit_solution(17282354931980316428)
XLA Ops:
  8.8 22.4 %copy.16 = bf16[512,16384]{0,1:T(8,128)(2,1)} copy(bf16[512,16384]{1,0:T(8,128)(2,1)} %param.7) | data formatting | bytes 33554432 | tf_op args[3]
  31.2 11.9 %gather_fusion = bf16[1024,512]{1,0:T(8,128)(2,1)S(1)} fusion(bf16[512,16384]{0,1:T(8,128)(2,1)} %copy.16, s32[1024]{0:T(1024)S(1)} %broadcast_clamp_fusion), kind=kCustom, calls=%fused_computation | custom fusion | bytes 2101248 | tf_op jit(solution)/shard_map/jit(_take)/gather | solution.py:12
  46.7 35.4 %psum.56 = f32[128]{0:T(128)S(1)} all-reduce(f32[128]{0:T(128)S(1)} %convert_reduce_fusion.6), channel_id=1, replica_groups=mesh['groups'=2,'state'=16] {'state'}, use_global_device_ids=true, to_apply=%region_1.2 | all-reduce | flops 128 | bytes 1024 | tf_op jit(solution)/shard_map/psum | solution.py:21
  82.1 7.6 %all-gather.8.cloned.1.call-done = bf16[128,8192]{1,0:T(8,128)(2,1)} async-done(((bf16[128,512]{1,0:T(8,128)(2,1)}), bf16[128,8192]{1,0:T(8,128)(2,1)}) %all-gather.8.cloned.1.call-update) | async-done | bytes 2097168 | tf_op jit(solution)/shard_map/all_gather | solution.py:20
  89.7 7.7 %convert_reduce_fusion.5 = (f32[128]{0:T(128)S(1)}, bf16[128,512]{1,0:T(8,128)(2,1)}, f32[128,512]{1,0:T(8,128)}) fusion(f32[512,128,8]{0,1,2:T(8,128)S(1)} %get-tuple-element.18, f32[128]{0:T(128)S(1)} %psum.56, bf16[128,8192]{1,0:T(8,128)(2,1)} %all-gather.8.cloned.1.call-done, bf16[512,8192]{1,0:T(8,128)(2,1)} %param.6), kind=kOutput, calls=%fused_computation.69 | convolution fusion | flops 1074069376 | bytes 11142144 | tf_op jit(solution)/shard_map/dot_general | solution.py:22
  97.4 32.3 %psum.57 = f32[128]{0:T(128)S(1)} all-reduce(f32[128]{0:T(128)S(1)} %get-tuple-element.16), channel_id=1, replica_groups=mesh['groups'=2,'state'=16] {'state'}, use_global_device_ids=true, to_apply=%region_3.4 | all-reduce | flops 128 | bytes 1024 | tf_op jit(solution)/shard_map/psum | solution.py:21
  129.7 8.1 %all-gather.10.cloned.1.call-done = bf16[128,8192]{1,0:T(8,128)(2,1)} async-done(((bf16[128,512]{1,0:T(8,128)(2,1)}), bf16[128,8192]{1,0:T(8,128)(2,1)}) %all-gather.10.cloned.1.call-update) | async-done | bytes 2097168 | tf_op jit(solution)/shard_map/all_gather | solution.py:20
  137.8 7.7 %convert_reduce_fusion.4 = (f32[128]{0:T(128)S(1)}, bf16[128,512]{1,0:T(8,128)(2,1)}, f32[128,512]{1,0:T(8,128)}) fusion(f32[512,128,8]{0,1,2:T(8,128)S(1)} %get-tuple-element.18, f32[128]{0:T(128)S(1)} %psum.57, bf16[128,8192]{1,0:T(8,128)(2,1)} %all-gather.10.cloned.1.call-done, bf16[512,8192]{1,0:T(8,128)(2,1)} %param.6), kind=kOutput, calls=%fused_computation.68 | convolution fusion | flops 1074069376 | bytes 11142144 | tf_op jit(solution)/shard_map/dot_general | solution.py:22
  145.6 31.7 %psum.58 = f32[128]{0:T(128)S(1)} all-reduce(f32[128]{0:T(128)S(1)} %get-tuple-element.14), channel_id=1, replica_groups=mesh['groups'=2,'state'=16] {'state'}, use_global_device_ids=true, to_apply=%region_5.6 | all-reduce | flops 128 | bytes 1024 | tf_op jit(solution)/shard_map/psum | solution.py:21
  177.3 8.5 %all-gather.12.cloned.1.call-done = bf16[128,8192]{1,0:T(8,128)(2,1)} async-done(((bf16[128,512]{1,0:T(8,128)(2,1)}), bf16[128,8192]{1,0:T(8,128)(2,1)}) %all-gather.12.cloned.1.call-update) | async-done | bytes 2097168 | tf_op jit(solution)/shard_map/all_gather | solution.py:20
  185.9 7.7 %convert_reduce_fusion.3 = (f32[128]{0:T(128)S(1)}, bf16[128,512]{1,0:T(8,128)(2,1)}, f32[128,512]{1,0:T(8,128)}) fusion(f32[512,128,8]{0,1,2:T(8,128)S(1)} %get-tuple-element.18, f32[128]{0:T(128)S(1)} %psum.58, bf16[128,8192]{1,0:T(8,128)(2,1)} %all-gather.12.cloned.1.call-done, bf16[512,8192]{1,0:T(8,128)(2,1)} %param.6), kind=kOutput, calls=%fused_computation.67 | convolution fusion | flops 1074069376 | bytes 11142144 | tf_op jit(solution)/shard_map/dot_general | solution.py:22
  193.6 32.3 %psum.59 = f32[128]{0:T(128)S(1)} all-reduce(f32[128]{0:T(128)S(1)} %get-tuple-element.12), channel_id=1, replica_groups=mesh['groups'=2,'state'=16] {'state'}, use_global_device_ids=true, to_apply=%region_7.8 | all-reduce | flops 128 | bytes 1024 | tf_op jit(solution)/shard_map/psum | solution.py:21
  226.0 8.0 %all-gather.14.cloned.1.call-done = bf16[128,8192]{1,0:T(8,128)(2,1)} async-done(((bf16[128,512]{1,0:T(8,128)(2,1)}), bf16[128,8192]{1,0:T(8,128)(2,1)}) %all-gather.14.cloned.1.call-update) | async-done | bytes 2097168 | tf_op jit(solution)/shard_map/all_gather | solution.py:20
  233.9 7.7 %convert_reduce_fusion.2 = (f32[128]{0:T(128)S(1)}, bf16[128,512]{1,0:T(8,128)(2,1)}, f32[128,512]{1,0:T(8,128)}) fusion(f32[512,128,8]{0,1,2:T(8,128)S(1)} %get-tuple-element.18, f32[128]{0:T(128)S(1)} %psum.59, bf16[128,8192]{1,0:T(8,128)(2,1)} %all-gather.14.cloned.1.call-done, bf16[512,8192]{1,0:T(8,128)(2,1)} %param.6), kind=kOutput, calls=%fused_computation.66 | convolution fusion | flops 1074069376 | bytes 11142144 | tf_op jit(solution)/shard_map/dot_general | solution.py:22
  241.7 32.2 %psum.60 = f32[128]{0:T(128)S(1)} all-reduce(f32[128]{0:T(128)S(1)} %get-tuple-element.10), channel_id=1, replica_groups=mesh['groups'=2,'state'=16] {'state'}, use_global_device_ids=true, to_apply=%region_9.10 | all-reduce | flops 128 | bytes 1024 | tf_op jit(solution)/shard_map/psum | solution.py:21
  273.9 8.1 %all-gather.16.cloned.1.call-done = bf16[128,8192]{1,0:T(8,128)(2,1)} async-done(((bf16[128,512]{1,0:T(8,128)(2,1)}), bf16[128,8192]{1,0:T(8,128)(2,1)}) %all-gather.16.cloned.1.call-update) | async-done | bytes 2097168 | tf_op jit(solution)/shard_map/all_gather | solution.py:20
  282.0 7.7 %convert_reduce_fusion.1 = (f32[128]{0:T(128)S(1)}, bf16[128,512]{1,0:T(8,128)(2,1)}, f32[128,512]{1,0:T(8,128)}) fusion(f32[512,128,8]{0,1,2:T(8,128)S(1)} %get-tuple-element.18, f32[128]{0:T(128)S(1)} %psum.60, bf16[128,8192]{1,0:T(8,128)(2,1)} %all-gather.16.cloned.1.call-done, bf16[512,8192]{1,0:T(8,128)(2,1)} %param.6), kind=kOutput, calls=%fused_computation.65 | convolution fusion | flops 1074069376 | bytes 11142144 | tf_op jit(solution)/shard_map/dot_general | solution.py:22
  289.8 32.1 %psum.61 = f32[128]{0:T(128)S(1)} all-reduce(f32[128]{0:T(128)S(1)} %get-tuple-element.8), channel_id=1, replica_groups=mesh['groups'=2,'state'=16] {'state'}, use_global_device_ids=true, to_apply=%region_11.12 | all-reduce | flops 128 | bytes 1024 | tf_op jit(solution)/shard_map/psum | solution.py:21
  321.9 8.1 %all-gather.18.cloned.1.call-done = bf16[128,8192]{1,0:T(8,128)(2,1)} async-done(((bf16[128,512]{1,0:T(8,128)(2,1)}), bf16[128,8192]{1,0:T(8,128)(2,1)}) %all-gather.18.cloned.1.call-update) | async-done | bytes 2097168 | tf_op jit(solution)/shard_map/all_gather | solution.py:20
  330.0 7.6 %convert_reduce_fusion = (f32[128]{0:T(128)S(1)}, bf16[128,512]{1,0:T(8,128)(2,1)}, f32[128,512]{1,0:T(8,128)}) fusion(f32[512,128,8]{0,1,2:T(8,128)} %copy-done.8, f32[128]{0:T(128)S(1)} %psum.61, bf16[128,8192]{1,0:T(8,128)(2,1)} %all-gather.18.cloned.1.call-done, bf16[512,8192]{1,0:T(8,128)(2,1)} %param.6), kind=kOutput, calls=%fused_computation.64 | convolution fusion | flops 1074069376 | bytes 11142144 | tf_op jit(solution)/shard_map/dot_general | solution.py:22
  339.7 32.0 %psum.62 = f32[128]{0:T(128)S(1)} all-reduce(f32[128]{0:T(128)S(1)} %get-tuple-element.6), channel_id=1, replica_groups=mesh['groups'=2,'state'=16] {'state'}, use_global_device_ids=true, to_apply=%region_13.14 | all-reduce | flops 128 | bytes 1024 | tf_op jit(solution)/shard_map/psum | solution.py:21
  378.1 7.7 %constant_dynamic-update-slice_fusion.1 = (f32[128,7,512]{2,0,1:T(8,128)S(1)}, f32[128,8,512]{2,0,1:T(8,128)}) fusion(f32[128]{0:T(128)S(1)} %psum.62, bf16[128,8192]{1,0:T(8,128)(2,1)} %all-gather.20.cloned.1.call-done, bf16[512,8192]{1,0:T(8,128)(2,1)} %param.6), kind=kOutput, calls=%fused_computation.81 | convolution fusion | flops 1073807360 | bytes 11010560 | tf_op jit(solution)/shard_map/dot_general | solution.py:22
  391.5 31.5 %psum.63 = f32[128,7]{0,1:T(8,128)S(1)} all-reduce(f32[128,7]{0,1:T(8,128)S(1)} %fusion), channel_id=1, replica_groups=mesh['groups'=2,'state'=16] {'state'}, use_global_device_ids=true, to_apply=%region_15.16 | all-reduce | flops 896 | bytes 7168 | tf_op jit(solution)/shard_map/psum | solution.py:38
  444.6 15.9 %multiply_multiply_fusion = f32[512,8192]{1,0:T(8,128)} fusion(bf16[512,8192]{1,0:T(8,128)(2,1)S(1)} %bitcast.172, bf16[896,512]{1,0:T(8,128)(2,1)S(1)} %fusion.34, bf16[896,8192]{1,0:T(8,128)(2,1)} %constant_dynamic-update-slice_fusion.2), kind=kOutput, calls=%fused_computation.1 | convolution fusion | flops 7528775680 | bytes 40763392 | tf_op jit(solution)/shard_map/dot_general | solution.py:46
  (89 shorter events, 41.0 us)
Async XLA Ops:
  7.2 82.5 %all-gather.8.cloned.1.call-start = ((), (), s32[]{:S(2)}) async-start(), calls=%async_computation | async-start | bytes 2228224 | tf_op jit(solution)/shard_map/all_gather | solution.py:20
  43.9 238.1 %copy-start.8 = (f32[512,128,8]{0,1,2:T(8,128)}, f32[512,128,8]{0,1,2:T(8,128)S(1)}, u32[]{:S(2)}) copy-start(f32[512,128,8]{0,1,2:T(8,128)S(1)} %get-tuple-element.18) | copy-start | bytes 6291460
  45.6 92.2 %all-gather.10.cloned.1.call-start = ((), (), s32[]{:S(2)}) async-start(), calls=%async_computation.1 | async-start | bytes 2228224 | tf_op jit(solution)/shard_map/all_gather | solution.py:20
  97.4 88.5 %all-gather.12.cloned.1.call-start = ((), (), s32[]{:S(2)}) async-start(), calls=%async_computation.2 | async-start | bytes 2228224 | tf_op jit(solution)/shard_map/all_gather | solution.py:20
  145.6 88.4 %all-gather.14.cloned.1.call-start = ((), (), s32[]{:S(2)}) async-start(), calls=%async_computation.3 | async-start | bytes 2228224 | tf_op jit(solution)/shard_map/all_gather | solution.py:20
  193.6 88.4 %all-gather.16.cloned.1.call-start = ((), (), s32[]{:S(2)}) async-start(), calls=%async_computation.4 | async-start | bytes 2228224 | tf_op jit(solution)/shard_map/all_gather | solution.py:20
  241.6 88.4 %all-gather.18.cloned.1.call-start = ((), (), s32[]{:S(2)}) async-start(), calls=%async_computation.5 | async-start | bytes 2228224 | tf_op jit(solution)/shard_map/all_gather | solution.py:20
  289.7 88.4 %all-gather.20.cloned.1.call-start = ((), (), s32[]{:S(2)}) async-start(), calls=%async_computation.6 | async-start | bytes 2228224 | tf_op jit(solution)/shard_map/all_gather | solution.py:20
  321.9 15.8 %copy-start.7 = (f32[128,8,512]{2,1,0:T(8,128)S(1)}, f32[128,8,512]{2,1,0:T(8,128)}, u32[]{:S(2)}) copy-start(f32[128,8,512]{2,1,0:T(8,128)} %param.4) | copy-start | bytes 6291460
  378.1 7.7 %copy-start.17 = (f32[128,512]{1,0:T(8,128)S(1)}, f32[128,512]{1,0:T(8,128)}, u32[]{:S(2)}) copy-start(f32[128,512]{1,0:T(8,128)} %get-tuple-element.53) | copy-start | bytes 786436
  378.1 8.5 %copy-start.16 = (f32[128,512]{1,0:T(8,128)S(1)}, f32[128,512]{1,0:T(8,128)}, u32[]{:S(2)}) copy-start(f32[128,512]{1,0:T(8,128)} %get-tuple-element.52) | copy-start | bytes 786436
  378.1 9.2 %copy-start.15 = (f32[128,512]{1,0:T(8,128)S(1)}, f32[128,512]{1,0:T(8,128)}, u32[]{:S(2)}) copy-start(f32[128,512]{1,0:T(8,128)} %get-tuple-element.51) | copy-start | bytes 786436
  385.9 3.0 copy-start.13
  385.9 3.7 copy-start.12
  423.8 4.2 copy-start.11
  423.8 4.3 copy-start.10
  429.6 2.3 copy-start.5
  431.9 2.3 copy-start.4
  434.3 2.3 copy-start.3
  434.3 3.8 copy-start.2
  436.6 7.3 %slice-start = ((s8[8388608]{0:T(1024)(128)(4,1)}), s8[4194304]{0:T(1024)(128)(4,1)S(1)}, s32[]{:S(2)}) async-start(s8[8388608]{0:T(1024)(128)(4,1)} %bitcast.171), calls=%async_computation.7 | async-start | bytes 8388608
  438.1 2.8 copy-start.1
  438.1 4.3 copy-start
  440.9 3.7 slice-start.1
  (3 other events, 4.8 us)
Sparse Core Ops, SparseCore 0:
  45.7 43.8 all-gather.7
  97.5 40.2 all-gather.9
  145.7 40.1 all-gather.11
  193.7 40.1 all-gather.13
  241.8 40.1 all-gather.15
  289.8 40.1 all-gather.17
  337.8 40.2 all-gather.19
where the time goes:
time: 468 us; the launch traced here: 467 us
  blocking collectives  260 us (56%)
  matrix products  69.7 us (15%)
  local copies, waits for them, and re-layouts  64.2 us (14%)
  waiting for transfers between devices  55 us (12%)
  between operations  14.3 us (3%)
    psum x7, blocking collectives, on_device(): scale_sum = lax.psum(jnp.sum(weighted.astype(jnp.float32), axis=1), 'state')  228 us
    all_gather x7, waiting for transfers between devices, on_device(): whole = lax.all_gather(weighted, 'state', axis=1, tiled=True)  54.9 us
    dot_general x7, matrix products, on_device(): lax.dot_general(whole, transition, (((1,), (1,)), ((), ())), preferred_el...  53.8 us
    unnamed x54, local copies, waits for them, and re-layouts  46.6 us
    psum x1, blocking collectives, on_device(): norm_sums = lax.psum(partial_norms, 'state')  31.5 us
    dot_general x1, matrix products, on_device(): lax.dot_general(share_mat, vector_mat, (((0,), (0,)), ((), ())), preferre...  15.9 us
    gather x1, local copies, waits for them, and re-layouts, on_device(): jnp.take(emission, token_ids.reshape(-1), axis=1).astype(jnp.float32)  11.9 us
  transfers between devices with their start and end apart: 7, of which 7 were waited for; matrix products, arithmetic and copies ran while one was open for 1% of the time, Pallas kernels for 0%

commit v1 on v0

--- a/solution.py
+++ b/solution.py
@@ -2,6 +2,28 @@
 import jax.numpy as jnp
 from jax import lax
 from jax.sharding import PartitionSpec as P
+
+
+def joined_along(parts, dim):
+    parts = jnp.moveaxis(parts, 0, dim)
+    shape = parts.shape
+    return parts.reshape(*shape[:dim], shape[dim] * shape[dim + 1], *shape[dim + 2 :])
+
+
+def gather_around(x, axis, dim):
+    size = lax.axis_size(axis)
+    pairs = [(i, (i + 1) % size) for i in range(size)]
+    back = [(b, a) for a, b in pairs]
+    lower, upper = ([], [])
+    for step in range(size - 1):
+        if step % 2 == 0:
+            lower.append(lax.ppermute(lower[-1] if lower else x, axis, pairs))
+        else:
+            upper.append(lax.ppermute(upper[-1] if upper else x, axis, back))
+    blocks = jnp.stack([*lower[::-1], x, *upper])
+    shift = lax.axis_index(axis) - len(lower)
+    blocks = blocks[(jnp.arange(size) - shift) % size]
+    return joined_along(blocks, dim)
 
 
 def on_device(forward_probs, token_ids, transition, emission):
@@ -17,7 +39,7 @@
     stored = []
     scales = []
     for t in range(step_count - 2, -1, -1):
-        whole = lax.all_gather(weighted, "state", axis=1, tiled=True)
+        whole = gather_around(weighted, "state", 1)
         scale_sum = lax.psum(jnp.sum(weighted.astype(jnp.float32), axis=1), "state")
         product = lax.dot_general(
             whole, transition, (((1,), (1,)), ((), ())), preferred_element_type=jnp.float32

time: 468 us -> 933 us (1.99)
  starting transfers between devices: 0.29 us -> 188 us
  local copies, waits for them, and re-layouts: 64.2 us -> 213 us
  waiting for transfers between devices: 55 us -> 163 us
  matrix products: 69.7 us -> 82.6 us
  between operations: 14.3 us -> 1.7 us
  blocking collectives: 260 us -> 271 us
    ppermute x0 -> x105, starting transfers between devices: none -> 188 us  [the longest x49 184 us: gather_around(): upper.append(lax.ppermute(upper[-1] if upper else x, axis, back))]
    ppermute x0 -> x105, waiting for transfers between devices: none -> 163 us  [the longest x56 162 us: gather_around(): lower.append(lax.ppermute(lower[-1] if lower else x, axis, pairs))]
    unnamed x54 -> x229, local copies, waits for them, and re-layouts: 46.6 us -> 142 us
    all_gather x7 -> x0, waiting for transfers between devices: 54.9 us -> none  [on_device(): whole = lax.all_gather(weighted, 'state', axis=1, tiled=True)]
    transpose x0 -> x7, local copies, waits for them, and re-layouts: none -> 26.5 us  [joined_along(): parts = jnp.moveaxis(parts, 0, dim)]
    gather x0 -> x7, local copies, waits for them, and re-layouts: none -> 23.5 us  [gather_around(): blocks = blocks[(jnp.arange(size) - shift) % size]]
    psum x7, blocking collectives: 228 us -> 241 us  [on_device(): scale_sum = lax.psum(jnp.sum(weighted.astype(jnp.float32), axis=1), 'state')]
    dot_general x1, matrix products: 15.9 us -> 27.7 us  [on_device(): lax.dot_general(share_mat, vector_mat, (((0,), (0,)), ((), ())), preferre...]
  transfers between devices with their start and end apart: 7 -> 105, of which waited for: 7 -> 49; matrix products, arithmetic and copies ran while one was open for 1% -> 10% of each run, Pallas kernels for 0% -> 0%
where the time goes in v1:
time: 933 us; the launch traced here: 924 us
  blocking collectives  271 us (29%)
  local copies, waits for them, and re-layouts  213 us (23%)
  starting transfers between devices  188 us (20%)
  waiting for transfers between devices  163 us (17%)
  matrix products  82.6 us (9%)
    psum x7, blocking collectives, on_device(): scale_sum = lax.psum(jnp.sum(weighted.astype(jnp.float32), axis=1), 'state')  241 us
    ppermute x49, starting transfers between devices, gather_around(): upper.append(lax.ppermute(upper[-1] if upper else x, axis, back))  184 us
    ppermute x56, waiting for transfers between devices, gather_around(): lower.append(lax.ppermute(lower[-1] if lower else x, axis, pairs))  162 us
    unnamed x229, local copies, waits for them, and re-layouts  142 us
    dot_general x7, matrix products, on_device(): lax.dot_general(whole, transition, (((1,), (1,)), ((), ())), preferred_el...  54.9 us
    psum x1, blocking collectives, on_device(): norm_sums = lax.psum(partial_norms, 'state')  30 us
    dot_general x1, matrix products, on_device(): lax.dot_general(share_mat, vector_mat, (((0,), (0,)), ((), ())), preferre...  27.7 us
    transpose x7, local copies, waits for them, and re-layouts, joined_along(): parts = jnp.moveaxis(parts, 0, dim)  26.5 us
  transfers between devices with their start and end apart: 105, of which 49 were waited for; matrix products, arithmetic and copies ran while one was open for 10% of the time, Pallas kernels for 0%

profile of v1, /device:TPU:0, one launch (start us, length us, event | category | flops | bytes accessed | tf_op | source)
XLA Modules:
  0.0 923.6 jit_solution(13781346332803504860)
XLA Ops:
  2.2 22.4 %copy.16 = bf16[512,16384]{0,1:T(8,128)(2,1)} copy(bf16[512,16384]{1,0:T(8,128)(2,1)} %param.7) | data formatting | bytes 33554432 | tf_op args[3]
  24.7 11.9 %gather_fusion = bf16[1024,512]{1,0:T(8,128)(2,1)S(1)} fusion(bf16[512,16384]{0,1:T(8,128)(2,1)} %copy.16, s32[1024]{0:T(1024)S(1)} %broadcast_clamp_fusion), kind=kCustom, calls=%fused_computation | custom fusion | bytes 2101248 | tf_op jit(solution)/shard_map/jit(_take)/gather | solution.py:34
  39.2 7.6 collective-permute-done
  89.9 34.0 %psum.56 = f32[128]{0:T(128)S(1)} all-reduce(f32[128]{0:T(128)S(1)} %convert_reduce_fusion.6), channel_id=1, replica_groups=mesh['groups'=2,'state'=16] {'state'}, use_global_device_ids=true, to_apply=%region_1.2 | all-reduce | flops 128 | bytes 1024 | tf_op jit(solution)/shard_map/psum | solution.py:43
  135.9 7.0 convert_reduce_fusion.5
  143.4 6.6 collective-permute-done.15
  193.2 34.0 %psum.57 = f32[128]{0:T(128)S(1)} all-reduce(f32[128]{0:T(128)S(1)} %get-tuple-element.16), channel_id=1, replica_groups=mesh['groups'=2,'state'=16] {'state'}, use_global_device_ids=true, to_apply=%region_3.4 | all-reduce | flops 128 | bytes 1024 | tf_op jit(solution)/shard_map/psum | solution.py:43
  249.5 8.1 convert_reduce_fusion.4
  258.1 6.6 collective-permute-done.30
  307.9 34.1 %psum.58 = f32[128]{0:T(128)S(1)} all-reduce(f32[128]{0:T(128)} %get-tuple-element.14), channel_id=1, replica_groups=mesh['groups'=2,'state'=16] {'state'}, use_global_device_ids=true, to_apply=%region_5.6 | all-reduce | flops 128 | bytes 1024 | tf_op jit(solution)/shard_map/psum | solution.py:43
  363.9 8.1 convert_reduce_fusion.3
  372.5 6.6 collective-permute-done.45
  422.3 34.7 %psum.59 = f32[128]{0:T(128)} all-reduce(f32[128]{0:T(128)} %get-tuple-element.12), channel_id=1, replica_groups=mesh['groups'=2,'state'=16] {'state'}, use_global_device_ids=true, to_apply=%region_7.8 | all-reduce | flops 128 | bytes 1024 | tf_op jit(solution)/shard_map/psum | solution.py:43
  478.7 8.1 convert_reduce_fusion.2
  487.3 6.6 collective-permute-done.60
  537.3 34.7 %psum.60 = f32[128]{0:T(128)} all-reduce(f32[128]{0:T(128)} %get-tuple-element.10), channel_id=1, replica_groups=mesh['groups'=2,'state'=16] {'state'}, use_global_device_ids=true, to_apply=%region_9.10 | all-reduce | flops 128 | bytes 1024 | tf_op jit(solution)/shard_map/psum | solution.py:43
  593.8 8.1 convert_reduce_fusion.1
  602.4 6.6 collective-permute-done.75
  652.2 34.7 %psum.61 = f32[128]{0:T(128)} all-reduce(f32[128]{0:T(128)} %get-tuple-element.8), channel_id=1, replica_groups=mesh['groups'=2,'state'=16] {'state'}, use_global_device_ids=true, to_apply=%region_11.12 | all-reduce | flops 128 | bytes 1024 | tf_op jit(solution)/shard_map/psum | solution.py:43
  708.7 8.3 convert_reduce_fusion
  769.3 34.5 %psum.62 = f32[128]{0:T(128)} all-reduce(f32[128]{0:T(128)} %get-tuple-element.6), channel_id=1, replica_groups=mesh['groups'=2,'state'=16] {'state'}, use_global_device_ids=true, to_apply=%region_13.14 | all-reduce | flops 128 | bytes 1024 | tf_op jit(solution)/shard_map/psum | solution.py:43
  834.6 7.1 constant_dynamic-update-slice_fusion.126
  847.5 30.0 %psum.63 = f32[128,7]{0,1:T(8,128)S(1)} all-reduce(f32[128,7]{0,1:T(8,128)S(1)} %fusion), channel_id=1, replica_groups=mesh['groups'=2,'state'=16] {'state'}, use_global_device_ids=true, to_apply=%region_15.16 | all-reduce | flops 896 | bytes 7168 | tf_op jit(solution)/shard_map/psum | solution.py:60
  895.7 27.7 %multiply_multiply_fusion = f32[512,8192]{1,0:T(8,128)} fusion(bf16[512,8192]{1,0:T(8,128)(2,1)} %param.6, bf16[896,512]{1,0:T(8,128)(2,1)S(1)} %constant_dynamic-update-slice_fusion.127, bf16[896,8192]{0,1:T(8,128)(2,1)} %constant_dynamic-update-slice_fusion.134), kind=kOutput, calls=%fused_computation.8 | convolution fusion | flops 7528775680 | bytes 40763392 | tf_op jit(solution)/shard_map/dot_general | solution.py:68
  (475 shorter events, 493.6 us)
Async XLA Ops:
  38.7 8.2 collective-permute-start
  75.5 7.3 collective-permute-start.12
  82.9 41.0 %collective-permute-start.13 = (bf16[128,512]{1,0:T(8,128)(2,1)S(1)}, bf16[128,512]{1,0:T(8,128)(2,1)}, u32[]{:S(2)}, u32[]{:S(2)}) collective-permute-start(bf16[128,512]{1,0:T(8,128)(2,1)S(1)} %collective-permute-done.12), channel_id=1, source_target_pairs={{1,0},{2,1},{3,2},{4,3},{5,4},{6,5},{7,6},{8,7},{9,8},{10,9},{11,1... | collective-permute-start | bytes 393224 | tf_op jit(solution)/shard_map/ppermute | solution.py:22
  89.9 34.2 %collective-permute-start.7 = (bf16[128,512]{1,0:T(8,128)(2,1)S(1)}, bf16[128,512]{1,0:T(8,128)(2,1)}, u32[]{:S(2)}, u32[]{:S(2)}) collective-permute-start(bf16[128,512]{1,0:T(8,128)(2,1)S(1)} %collective-permute-done.6), channel_id=1, source_target_pairs={{0,1},{1,2},{2,3},{3,4},{4,5},{5,6},{6,7},{7,8},{8,9},{9,10},{10,1... | collective-permute-start | bytes 393224 | tf_op jit(solution)/shard_map/ppermute | solution.py:20
  186.6 40.6 %collective-permute-start.28 = (bf16[128,512]{1,0:T(8,128)(2,1)S(1)}, bf16[128,512]{1,0:T(8,128)(2,1)}, u32[]{:S(2)}, u32[]{:S(2)}) collective-permute-start(bf16[128,512]{1,0:T(8,128)(2,1)S(1)} %collective-permute-done.27), channel_id=1, source_target_pairs={{1,0},{2,1},{3,2},{4,3},{5,4},{6,5},{7,6},{8,7},{9,8},{10,9},{11,1... | collective-permute-start | bytes 393224 | tf_op jit(solution)/shard_map/ppermute | solution.py:22
  193.2 34.5 %collective-permute-start.22 = (bf16[128,512]{1,0:T(8,128)(2,1)}, bf16[128,512]{1,0:T(8,128)(2,1)}, u32[]{:S(2)}, u32[]{:S(2)}) collective-permute-start(bf16[128,512]{1,0:T(8,128)(2,1)} %collective-permute-done.21), channel_id=1, source_target_pairs={{0,1},{1,2},{2,3},{3,4},{4,5},{5,6},{6,7},{7,8},{8,9},{9,10},{10,1... | collective-permute-start | bytes 393224 | tf_op jit(solution)/shard_map/ppermute | solution.py:20
  227.2 14.1 %collective-permute-start.29 = (bf16[128,512]{1,0:T(8,128)(2,1)}, bf16[128,512]{1,0:T(8,128)(2,1)S(1)}, u32[]{:S(2)}, u32[]{:S(2)}) collective-permute-start(bf16[128,512]{1,0:T(8,128)(2,1)} %collective-permute-done.28), channel_id=1, source_target_pairs={{1,0},{2,1},{3,2},{4,3},{5,4},{6,5},{7,6},{8,7},{9,8},{10,9},{11,1... | collective-permute-start | bytes 393224 | tf_op jit(solution)/shard_map/ppermute | solution.py:22
  301.3 40.7 %collective-permute-start.43 = (bf16[128,512]{1,0:T(8,128)(2,1)S(1)}, bf16[128,512]{1,0:T(8,128)(2,1)}, u32[]{:S(2)}, u32[]{:S(2)}) collective-permute-start(bf16[128,512]{1,0:T(8,128)(2,1)S(1)} %collective-permute-done.42), channel_id=1, source_target_pairs={{1,0},{2,1},{3,2},{4,3},{5,4},{6,5},{7,6},{8,7},{9,8},{10,9},{11,1... | collective-permute-start | bytes 393224 | tf_op jit(solution)/shard_map/ppermute | solution.py:22
  307.9 34.2 %collective-permute-start.37 = (bf16[128,512]{1,0:T(8,128)(2,1)}, bf16[128,512]{1,0:T(8,128)(2,1)}, u32[]{:S(2)}, u32[]{:S(2)}) collective-permute-start(bf16[128,512]{1,0:T(8,128)(2,1)} %collective-permute-done.36), channel_id=1, source_target_pairs={{0,1},{1,2},{2,3},{3,4},{4,5},{5,6},{6,7},{7,8},{8,9},{9,10},{10,1... | collective-permute-start | bytes 393224 | tf_op jit(solution)/shard_map/ppermute | solution.py:20
  342.1 13.6 %collective-permute-start.44 = (bf16[128,512]{1,0:T(8,128)(2,1)}, bf16[128,512]{1,0:T(8,128)(2,1)S(1)}, u32[]{:S(2)}, u32[]{:S(2)}) collective-permute-start(bf16[128,512]{1,0:T(8,128)(2,1)} %collective-permute-done.43), channel_id=1, source_target_pairs={{1,0},{2,1},{3,2},{4,3},{5,4},{6,5},{7,6},{8,7},{9,8},{10,9},{11,1... | collective-permute-start | bytes 393224 | tf_op jit(solution)/shard_map/ppermute | solution.py:22
  415.7 41.3 %collective-permute-start.58 = (bf16[128,512]{1,0:T(8,128)(2,1)S(1)}, bf16[128,512]{1,0:T(8,128)(2,1)}, u32[]{:S(2)}, u32[]{:S(2)}) collective-permute-start(bf16[128,512]{1,0:T(8,128)(2,1)S(1)} %collective-permute-done.57), channel_id=1, source_target_pairs={{1,0},{2,1},{3,2},{4,3},{5,4},{6,5},{7,6},{8,7},{9,8},{10,9},{11,1... | collective-permute-start | bytes 393224 | tf_op jit(solution)/shard_map/ppermute | solution.py:22
  422.3 34.7 %collective-permute-start.52 = (bf16[128,512]{1,0:T(8,128)(2,1)}, bf16[128,512]{1,0:T(8,128)(2,1)}, u32[]{:S(2)}, u32[]{:S(2)}) collective-permute-start(bf16[128,512]{1,0:T(8,128)(2,1)} %collective-permute-done.51), channel_id=1, source_target_pairs={{0,1},{1,2},{2,3},{3,4},{4,5},{5,6},{6,7},{7,8},{8,9},{9,10},{10,1... | collective-permute-start | bytes 393224 | tf_op jit(solution)/shard_map/ppermute | solution.py:20
  457.0 13.6 %collective-permute-start.59 = (bf16[128,512]{1,0:T(8,128)(2,1)}, bf16[128,512]{1,0:T(8,128)(2,1)S(1)}, u32[]{:S(2)}, u32[]{:S(2)}) collective-permute-start(bf16[128,512]{1,0:T(8,128)(2,1)} %collective-permute-done.58), channel_id=1, source_target_pairs={{1,0},{2,1},{3,2},{4,3},{5,4},{6,5},{7,6},{8,7},{9,8},{10,9},{11,1... | collective-permute-start | bytes 393224 | tf_op jit(solution)/shard_map/ppermute | solution.py:22
  508.3 7.4 collective-permute-start.70
  515.5 7.4 collective-permute-start.64
  530.7 41.3 %collective-permute-start.73 = (bf16[128,512]{1,0:T(8,128)(2,1)S(1)}, bf16[128,512]{1,0:T(8,128)(2,1)}, u32[]{:S(2)}, u32[]{:S(2)}) collective-permute-start(bf16[128,512]{1,0:T(8,128)(2,1)S(1)} %collective-permute-done.72), channel_id=1, source_target_pairs={{1,0},{2,1},{3,2},{4,3},{5,4},{6,5},{7,6},{8,7},{9,8},{10,9},{11,1... | collective-permute-start | bytes 393224 | tf_op jit(solution)/shard_map/ppermute | solution.py:22
  537.3 34.7 %collective-permute-start.67 = (bf16[128,512]{1,0:T(8,128)(2,1)}, bf16[128,512]{1,0:T(8,128)(2,1)}, u32[]{:S(2)}, u32[]{:S(2)}) collective-permute-start(bf16[128,512]{1,0:T(8,128)(2,1)} %collective-permute-done.66), channel_id=1, source_target_pairs={{0,1},{1,2},{2,3},{3,4},{4,5},{5,6},{6,7},{7,8},{8,9},{9,10},{10,1... | collective-permute-start | bytes 393224 | tf_op jit(solution)/shard_map/ppermute | solution.py:20
  572.0 13.6 %collective-permute-start.74 = (bf16[128,512]{1,0:T(8,128)(2,1)}, bf16[128,512]{1,0:T(8,128)(2,1)S(1)}, u32[]{:S(2)}, u32[]{:S(2)}) collective-permute-start(bf16[128,512]{1,0:T(8,128)(2,1)} %collective-permute-done.73), channel_id=1, source_target_pairs={{1,0},{2,1},{3,2},{4,3},{5,4},{6,5},{7,6},{8,7},{9,8},{10,9},{11,1... | collective-permute-start | bytes 393224 | tf_op jit(solution)/shard_map/ppermute | solution.py:22
  645.7 41.3 %collective-permute-start.88 = (bf16[128,512]{1,0:T(8,128)(2,1)S(1)}, bf16[128,512]{1,0:T(8,128)(2,1)}, u32[]{:S(2)}, u32[]{:S(2)}) collective-permute-start(bf16[128,512]{1,0:T(8,128)(2,1)S(1)} %collective-permute-done.87), channel_id=1, source_target_pairs={{1,0},{2,1},{3,2},{4,3},{5,4},{6,5},{7,6},{8,7},{9,8},{10,9},{11,1... | collective-permute-start | bytes 393224 | tf_op jit(solution)/shard_map/ppermute | solution.py:22
  652.2 34.7 %collective-permute-start.82 = (bf16[128,512]{1,0:T(8,128)(2,1)}, bf16[128,512]{1,0:T(8,128)(2,1)}, u32[]{:S(2)}, u32[]{:S(2)}) collective-permute-start(bf16[128,512]{1,0:T(8,128)(2,1)} %collective-permute-done.81), channel_id=1, source_target_pairs={{0,1},{1,2},{2,3},{3,4},{4,5},{5,6},{6,7},{7,8},{8,9},{9,10},{10,1... | collective-permute-start | bytes 393224 | tf_op jit(solution)/shard_map/ppermute | solution.py:20
  686.9 13.6 %collective-permute-start.89 = (bf16[128,512]{1,0:T(8,128)(2,1)}, bf16[128,512]{1,0:T(8,128)(2,1)S(1)}, u32[]{:S(2)}, u32[]{:S(2)}) collective-permute-start(bf16[128,512]{1,0:T(8,128)(2,1)} %collective-permute-done.88), channel_id=1, source_target_pairs={{1,0},{2,1},{3,2},{4,3},{5,4},{6,5},{7,6},{8,7},{9,8},{10,9},{11,1... | collective-permute-start | bytes 393224 | tf_op jit(solution)/shard_map/ppermute | solution.py:22
  760.1 43.8 %collective-permute-start.103 = (bf16[128,512]{1,0:T(8,128)(2,1)}, bf16[128,512]{1,0:T(8,128)(2,1)}, u32[]{:S(2)}, u32[]{:S(2)}) collective-permute-start(bf16[128,512]{1,0:T(8,128)(2,1)} %collective-permute-done.102), channel_id=1, source_target_pairs={{1,0},{2,1},{3,2},{4,3},{5,4},{6,5},{7,6},{8,7},{9,8},{10,9},{11,1... | collective-permute-start | bytes 393224 | tf_op jit(solution)/shard_map/ppermute | solution.py:22
  767.3 36.8 %collective-permute-start.97 = (bf16[128,512]{1,0:T(8,128)(2,1)}, bf16[128,512]{1,0:T(8,128)(2,1)}, u32[]{:S(2)}, u32[]{:S(2)}) collective-permute-start(bf16[128,512]{1,0:T(8,128)(2,1)} %collective-permute-done.96), channel_id=1, source_target_pairs={{0,1},{1,2},{2,3},{3,4},{4,5},{5,6},{6,7},{7,8},{8,9},{9,10},{10,1... | collective-permute-start | bytes 393224 | tf_op jit(solution)/shard_map/ppermute | solution.py:20
  803.9 19.3 %collective-permute-start.104 = (bf16[128,512]{1,0:T(8,128)(2,1)}, bf16[128,512]{1,0:T(8,128)(2,1)S(1)}, u32[]{:S(2)}, u32[]{:S(2)}) collective-permute-start(bf16[128,512]{1,0:T(8,128)(2,1)} %collective-permute-done.103), channel_id=1, source_target_pairs={{1,0},{2,1},{3,2},{4,3},{5,4},{6,5},{7,6},{8,7},{9,8},{10,9},{11,1... | collective-permute-start | bytes 393224 | tf_op jit(solution)/shard_map/ppermute | solution.py:22
  (136 other events, 1612.5 us)
